TPU v7x, 32 devices: a whole 2x2x4 slice. The times are simulated.
32 devices in a mesh: grp: 4 (over z), band: 8 (over y, x, core).
Axes of the slice: x: 2, y: 2, z: 4, core: 2. Of those that a mesh axis runs over, the one named last changes fastest.
Arguments:
- orbitals: float32 [18432, 512], P('grp', 'band'), may hold values from -6 to 6
- requests: int32 [32, 6], replicated, may hold values from -1 to 11, as said below
- coulomb: float32 [96, 1536, 1536], P(('grp', 'band')), may hold values from -0.001953125 to 0.001953125
Outputs:
- exchange_rows: float32 [18432, 512], P('grp', 'band')
Inputs may be any that keep to these rules, and one draw needn't show every extreme that they name: `requests`: entries 2q and 2q + 1 of row d are the two blocks of slot q of device d, the first not above the second, or both -1 for an empty slot; every pair of the 12 blocks, a block with itself included, stands in exactly one slot.
All inputs are finite; a program needn't handle non-finite values.
Results may differ from a plain program's by a relative error of at most 0.0003.
Values sent between devices are 32-bit elements; how exact they have to be, the bound alone decides.
No kernel may reach another device: no remote copies, remote signals or barrier semaphores. Data moves between devices by JAX's collectives and lax.ppermute only.
A program may use at most 256 MiB of HBM per device.

v0:
```python
import jax
import jax.numpy as jnp
from jax import lax
from jax.sharding import PartitionSpec as P


def slot_work(first_block, second_block, coulomb_tile, diagonal):
    density = jnp.dot(
        first_block,
        second_block.T,
        precision=lax.Precision.HIGHEST,
        preferred_element_type=jnp.float32,
    )
    symmetric = jnp.where(diagonal, 0.5 * (coulomb_tile + coulomb_tile.T), coulomb_tile)
    kernel = density * symmetric
    onto_first = jnp.dot(
        kernel, second_block, precision=lax.Precision.HIGHEST, preferred_element_type=jnp.float32
    )
    onto_second = jnp.dot(
        kernel.T, first_block, precision=lax.Precision.HIGHEST, preferred_element_type=jnp.float32
    )
    onto_second = onto_second * jnp.where(diagonal, 0.0, 1.0)
    return jnp.stack([onto_first, onto_second], 0)


def body(orbitals, requests, coulomb):
    group_count = lax.axis_size("grp")
    band_count = lax.axis_size("band")
    devices = group_count * band_count
    blk = coulomb.shape[1]
    col_width = orbitals.shape[1]
    orbital_width = col_width * band_count
    piece_rows = blk // devices
    all_points = lax.all_gather(orbitals, "grp", axis=0, tiled=True)
    block_count = all_points.shape[0] // (devices * piece_rows)
    blocks = (
        all_points.reshape(devices, block_count, piece_rows, col_width)
        .transpose(1, 0, 2, 3)
        .reshape(block_count, blk, col_width)
    )
    request_count = requests.shape[1]
    group_index = lax.axis_index("grp")
    band_index = lax.axis_index("band")
    group_requests = lax.dynamic_slice_in_dim(requests, group_index * band_count, band_count, 0)
    live = (group_requests >= 0).astype(jnp.float32)
    outgoing = jnp.take(blocks, jnp.maximum(group_requests, 0), axis=0) * live[:, :, None, None]
    arrived = lax.all_to_all(outgoing, "band", split_axis=0, concat_axis=0, tiled=True)
    fetched = arrived.transpose(1, 2, 0, 3).reshape(request_count // 2, 2, blk, orbital_width)
    own_pairs = lax.dynamic_index_in_dim(group_requests, band_index, 0, keepdims=False).reshape(
        request_count // 2, 2
    )
    diagonal = own_pairs[:, 0] == own_pairs[:, 1]

    def per_slot(slot_item):
        pair_rows, coulomb_tile, diag_flag = slot_item
        return slot_work(pair_rows[0], pair_rows[1], coulomb_tile, diag_flag)

    results = lax.map(per_slot, (fetched, coulomb, diagonal))
    outbound = results.reshape(request_count, blk, band_count, col_width).transpose(2, 0, 1, 3)
    returned = lax.all_to_all(outbound, "band", split_axis=0, concat_axis=0, tiled=True)
    one_hot = (
        group_requests[:, :, None] == jnp.arange(block_count, dtype=jnp.int32)[None, None, :]
    ).astype(jnp.float32)
    summed = jnp.einsum("srk,srpc->kpc", one_hot, returned, precision=lax.Precision.HIGHEST)
    summed = summed.reshape(block_count, group_count, band_count, piece_rows, col_width)
    mine = lax.psum_scatter(summed, "grp", scatter_dimension=1, tiled=True)
    mine = mine.reshape(block_count, band_count, piece_rows, col_width).transpose(1, 0, 2, 3)
    return mine.reshape(band_count * block_count * piece_rows, col_width)


def solution(mesh):
    placed = (P("grp", "band"), P(), P(("grp", "band"), None, None))
    return jax.shard_map(
        body, mesh=mesh, in_specs=placed, out_specs=P("grp", "band"), check_vma=False
    )
```

profile of v0, /device:TPU:0, one launch (start us, length us, event | category | flops | bytes accessed | tf_op | source)
XLA Modules:
  0.0 1245.0 jit_solution(937388461470944513)
XLA Ops:
  10.6 168.5 %all-gather.2.cloned.1.call-done = f32[18432,64]{1,0:T(8,128)} async-done(((f32[4608,64]{1,0:T(8,128)}), f32[18432,64]{1,0:T(8,128)}) %all-gather.2.cloned.1.call-update) | async-done | bytes 4718608 | tf_op jit(solution)/shard_map/all_gather | solution.py:34
  179.0 12.0 copy.38
  191.1 13.1 %reshape.38 = f32[12,1536,64]{1,2,0:T(8,128)} reshape(f32[12,32,48,64]{2,1,3,0:T(8,128)} %copy.38) | data formatting | bytes 9437184 | tf_op jit(solution)/shard_map/reshape | solution.py:39
  204.1 12.6 %gather_fusion = f32[48,1536,64]{1,2,0:T(8,128)} fusion(f32[12,1536,64]{1,2,0:T(8,128)} %reshape.38, s32[1024]{0:T(1024)S(1)} %pad_clamp_fusion), kind=kCustom, calls=%fused_computation | custom fusion | bytes 37748928 | tf_op jit(solution)/shard_map/jit(_take)/gather | solution.py:46
  216.8 13.2 %select_multiply_fusion = f32[8,6,1536,64]{2,3,1,0:T(8,128)} fusion(f32[8,6,1536,64]{2,3,1,0:T(8,128)} %bitcast.84, f32[8,6]{1,0:T(8,128)S(1)} %copy.40, pred[8,6]{1,0:T(8,128)(4,1)S(1)} %copy.36), kind=kLoop, calls=%fused_computation.18 | loop fusion | flops 9437184 | bytes 37748976 | tf_op jit(solution)/shard_map/mul | solution.py:46
  236.5 205.9 %all-to-all-done = f32[8,6,1536,64]{2,3,1,0:T(8,128)} async-done(((f32[8,6,1536,64]{2,3,1,0:T(8,128)}), f32[8,6,1536,64]{2,3,1,0:T(8,128)}, u32[]{:S(2)}, u32[]{:S(2)}) %all-to-all-start) | async-done | bytes 18874400 | tf_op jit(solution)/shard_map/all_to_all | solution.py:47
  442.4 12.6 %copy.41 = f32[6,1536,8,64]{1,3,2,0:T(8,128)} copy(f32[6,1536,8,64]{1,3,0,2:T(8,128)} %bitcast.12) | data formatting | bytes 37748736 | tf_op jit(solution)/shard_map/transpose | solution.py:48
  455.0 359.6 %while.10 = (s32[]{:T(128)}, f32[3,2,1536,512]{2,3,1,0:T(8,128)}, f32[3,2,1536,512]{2,3,1,0:T(8,128)}, pred[3]{0:T(512)(128)(4,1)S(1)}, f32[3,1536,1536]{2,1,0:T...) while((s32[]{:T(128)}, f32[3,2,1536,512]{2,3,1,0:T(8,128)}, ...), condition=%wide.region_1.2_spmd, body=%wide.region_0.1_spmd.sunk | while | flops 43498340352 | bytes 179310272 | solution.py:58
  493.6 22.7 %convolution_multiply_fusion.3 = f32[1536,1536]{1,0:T(8,128)S(1)} fusion(f32[1536,1536]{0,1:T(8,128)} %copy.64, pred[]{:T(512)} %bitcast.83, f32[3,2,1536,512]{2,3,1,0:T(8,128)} %get-tuple-element.113, s32[]{:T(128)} %get-tuple-element.101, s32[]{:T(128)S(6)} %add.38, f32[3,1536,1536]{2,1,0:T(8,128)} %get-tuple-element.115), kind=kOutput, calls=%fused_computation.1.clone.1 | convolution fusion | flops 14504951808 | bytes 34605060 | tf_op jit(solution)/shard_map/while/body/eval_jaxpr/dot_general | solution.py:8
  519.9 17.0 %convolution_bitcast_fusion.2 = f32[1,1536,512]{2,1,0:T(8,128)S(1)} fusion(f32[1536,1536]{1,0:T(8,128)S(1)} %convolution_multiply_fusion.3, f32[3,2,1536,512]{2,3,1,0:T(8,128)} %get-tuple-element.113, s32[]{:T(128)} %get-tuple-element.101, s32[]{:T(128)S(6)} %add.38), kind=kOutput, calls=%fused_computation.9.clone.1 | convolution fusion | flops 14495514624 | bytes 15729156 | tf_op jit(solution)/shard_map/while/body/eval_jaxpr/dot_general | solution.py:16
  537.4 32.9 %fusion.22 = f32[1,1536,512]{2,1,0:T(8,128)S(1)} fusion(f32[1536,1536]{1,0:T(8,128)} %copy-done, f32[3,2,1536,512]{2,3,1,0:T(8,128)} %get-tuple-element.113, s32[]{:T(128)} %get-tuple-element.101, f32[]{:T(128)S(6)} %select_n.45), kind=kOutput, calls=%fused_computation.8.clone.1 | convolution fusion | flops 14496301056 | bytes 15729156 | tf_op jit(solution)/shard_map/while/body/eval_jaxpr/dot_general | solution.py:19
  594.1 9.6 copy.64
  604.3 22.7 %convolution_multiply_fusion.3 = f32[1536,1536]{1,0:T(8,128)S(1)} fusion(f32[1536,1536]{0,1:T(8,128)} %copy.64, pred[]{:T(512)} %bitcast.83, f32[3,2,1536,512]{2,3,1,0:T(8,128)} %get-tuple-element.113, s32[]{:T(128)} %get-tuple-element.101, s32[]{:T(128)S(6)} %add.38, f32[3,1536,1536]{2,1,0:T(8,128)} %get-tuple-element.115), kind=kOutput, calls=%fused_computation.1.clone.1 | convolution fusion | flops 14504951808 | bytes 34605060 | tf_op jit(solution)/shard_map/while/body/eval_jaxpr/dot_general | solution.py:8
  630.6 17.0 %convolution_bitcast_fusion.2 = f32[1,1536,512]{2,1,0:T(8,128)S(1)} fusion(f32[1536,1536]{1,0:T(8,128)S(1)} %convolution_multiply_fusion.3, f32[3,2,1536,512]{2,3,1,0:T(8,128)} %get-tuple-element.113, s32[]{:T(128)} %get-tuple-element.101, s32[]{:T(128)S(6)} %add.38), kind=kOutput, calls=%fused_computation.9.clone.1 | convolution fusion | flops 14495514624 | bytes 15729156 | tf_op jit(solution)/shard_map/while/body/eval_jaxpr/dot_general | solution.py:16
  648.2 32.9 %fusion.22 = f32[1,1536,512]{2,1,0:T(8,128)S(1)} fusion(f32[1536,1536]{1,0:T(8,128)} %copy-done, f32[3,2,1536,512]{2,3,1,0:T(8,128)} %get-tuple-element.113, s32[]{:T(128)} %get-tuple-element.101, f32[]{:T(128)S(6)} %select_n.45), kind=kOutput, calls=%fused_computation.8.clone.1 | convolution fusion | flops 14496301056 | bytes 15729156 | tf_op jit(solution)/shard_map/while/body/eval_jaxpr/dot_general | solution.py:19
  715.1 22.7 %convolution_multiply_fusion.3 = f32[1536,1536]{1,0:T(8,128)S(1)} fusion(f32[1536,1536]{0,1:T(8,128)} %copy.64, pred[]{:T(512)} %bitcast.83, f32[3,2,1536,512]{2,3,1,0:T(8,128)} %get-tuple-element.113, s32[]{:T(128)} %get-tuple-element.101, s32[]{:T(128)S(6)} %add.38, f32[3,1536,1536]{2,1,0:T(8,128)} %get-tuple-element.115), kind=kOutput, calls=%fused_computation.1.clone.1 | convolution fusion | flops 14504951808 | bytes 34605060 | tf_op jit(solution)/shard_map/while/body/eval_jaxpr/dot_general | solution.py:8
  741.4 17.0 %convolution_bitcast_fusion.2 = f32[1,1536,512]{2,1,0:T(8,128)S(1)} fusion(f32[1536,1536]{1,0:T(8,128)S(1)} %convolution_multiply_fusion.3, f32[3,2,1536,512]{2,3,1,0:T(8,128)} %get-tuple-element.113, s32[]{:T(128)} %get-tuple-element.101, s32[]{:T(128)S(6)} %add.38), kind=kOutput, calls=%fused_computation.9.clone.1 | convolution fusion | flops 14495514624 | bytes 15729156 | tf_op jit(solution)/shard_map/while/body/eval_jaxpr/dot_general | solution.py:16
  759.0 32.9 %fusion.22 = f32[1,1536,512]{2,1,0:T(8,128)S(1)} fusion(f32[1536,1536]{1,0:T(8,128)} %copy-done, f32[3,2,1536,512]{2,3,1,0:T(8,128)} %get-tuple-element.113, s32[]{:T(128)} %get-tuple-element.101, f32[]{:T(128)S(6)} %select_n.45), kind=kOutput, calls=%fused_computation.8.clone.1 | convolution fusion | flops 14496301056 | bytes 15729156 | tf_op jit(solution)/shard_map/while/body/eval_jaxpr/dot_general | solution.py:19
  814.6 12.6 %copy.44 = f32[8,6,1536,64]{2,3,1,0:T(8,128)} copy(f32[8,6,1536,64]{2,3,0,1:T(8,128)} %bitcast.86) | data formatting | bytes 37748736 | tf_op jit(solution)/shard_map/transpose | solution.py:59
  827.2 210.7 %all_to_all.10 = f32[8,6,1536,64]{2,3,1,0:T(8,128)S(1)} all-to-all(f32[8,6,1536,64]{2,3,1,0:T(8,128)} %copy.44), channel_id=1, replica_groups=mesh['grp'=4,'band'=8] {'band'}, dimensions={0} | all-to-all | bytes 37748736 | tf_op jit(solution)/shard_map/all_to_all | solution.py:60
  1037.9 15.3 %fusion.8 = f32[12,1536,64]{1,0,2:T(8,128)} fusion(f32[8,6,1536,64]{2,3,1,0:T(8,128)S(1)} %all_to_all.10, s32[8,6]{0,1:T(8,128)S(1)} %copy-done.2), kind=kOutput, calls=%fused_computation.19 | convolution fusion | flops 679477824 | bytes 23593152 | tf_op jit(solution)/shard_map/srk,srpc->kpc/dot_general | solution.py:64
  1053.2 11.0 reshape.57
  1064.2 12.2 copy.47
  1076.5 157.9 %reduce-scatter.2.cloned.1.call-done = f32[12,1,8,48,64]{4,3,2,0,1:T(8,128)} async-done(((f32[12,4,8,48,64]{4,3,2,0,1:T(8,128)}), f32[12,1,8,48,64]{4,3,2,0,1:T(8,128)}) %reduce-scatter.2.cloned.1.call-update) | async-done | bytes 1179664 | tf_op jit(solution)/shard_map/reduce_scatter | solution.py:66
  (49 shorter events, 117.3 us)
Async XLA Ops:
  6.5 172.5 %all-gather.2.cloned.1.call-start = ((), (), s32[]{:S(2)}) async-start(), calls=%async_computation.3 | async-start | bytes 11796480 | tf_op jit(solution)/shard_map/all_gather | solution.py:34
  10.2 180.9 %copy-start.1 = (s32[8,6]{0,1:T(8,128)}, s32[8,6]{0,1:T(8,128)S(1)}, u32[]{:S(2)}) copy-start(s32[8,6]{0,1:T(8,128)S(1)} %get-tuple-element.59) | copy-start | bytes 580
  230.0 6.1 copy-start.3
  230.0 212.4 %all-to-all-start = ((f32[8,6,1536,64]{2,3,1,0:T(8,128)}), f32[8,6,1536,64]{2,3,1,0:T(8,128)}, u32[]{:S(2)}, u32[]{:S(2)}) async-start(f32[8,6,1536,64]{2,3,1,0:T(8,128)} %select_multiply_fusion), calls=%async_computation | async-start | bytes 37748736 | tf_op jit(solution)/shard_map/all_to_all | solution.py:47
  236.0 998.4 %reduce-scatter.2.cloned.1.call-start = ((), (), s32[]{:S(2)}) async-start(), calls=%async_computation.4 | async-start | bytes 11796480 | tf_op jit(solution)/shard_map/reduce_scatter | solution.py:66
  516.3 3.6 copy-start
  627.0 3.6 copy-start
  737.8 3.6 copy-start
  827.2 210.7 %copy-start.2 = (s32[8,6]{0,1:T(8,128)S(1)}, s32[8,6]{0,1:T(8,128)}, u32[]{:S(2)}) copy-start(s32[8,6]{0,1:T(8,128)} %copy-done.1) | copy-start | bytes 580
Sparse Core Ops, SparseCore 0:
  9.5 169.4 all-gather.1
  1076.6 157.7 reduce-scatter.1
where the time goes:
time: 1250 us; the launch traced here: 1240 us
  waiting for transfers between devices  532 us (43%)
  matrix products  233 us (19%)
  blocking collectives  211 us (17%)
  local copies, waits for them, and re-layouts  196 us (16%)
  loops' own time  29 us (2%)
  other arithmetic  24 us (2%)
  between operations  13.7 us (1%)
    all_to_all x1, blocking collectives, body(): lax.all_to_all(outbound, 'band', split_axis=0, concat_axis=0, tiled=True)  211 us
    all_to_all x1, waiting for transfers between devices, body(): lax.all_to_all(outgoing, 'band', split_axis=0, concat_axis=0, tiled=True)  206 us
    all_gather x1, waiting for transfers between devices, body(): all_points = lax.all_gather(orbitals, 'grp', axis=0, tiled=True)  168 us
    reduce_scatter x1, waiting for transfers between devices, body(): mine = lax.psum_scatter(summed, 'grp', scatter_dimension=1, tiled=True)  158 us
    dot_general x3, matrix products, slot_work(): jnp.dot(kernel.T, first_block, precision=lax.Precision.HIGHEST, preferred...  98.7 us
    dot_general x3, matrix products, slot_work(): jnp.dot(first_block, second_block.T, precision=lax.Precision.HIGHEST, pre...  68 us
    squeeze x6, local copies, waits for them, and re-layouts, body(): results = lax.map(per_slot, (fetched, coulomb, diagonal))  53.1 us
    dot_general x3, matrix products, slot_work(): jnp.dot(kernel, second_block, precision=lax.Precision.HIGHEST, preferred_...  51.1 us
  transfers between devices with their start and end apart: 3, of which 3 were waited for; matrix products, arithmetic and copies ran while one was open for 0% of the time, Pallas kernels for 0%

commit v1 on v0

--- a/solution.py
+++ b/solution.py
@@ -2,6 +2,17 @@
 import jax.numpy as jnp
 from jax import lax
 from jax.sharding import PartitionSpec as P
+
+
+def turned_line(shard, axis, dim):
+    size = lax.axis_size(axis)
+    right = [(i, (i + 1) % size) for i in range(size)]
+    terms = [shard]
+    for far in range(1, size):
+        terms = [lax.ppermute(terms[0], axis, right), *terms]
+    full = jnp.concatenate(terms, axis=dim)
+    places = (lax.axis_index(axis) + 1) * terms[-1].shape[dim]
+    return jnp.roll(full, places, axis=dim)
 
 
 def slot_work(first_block, second_block, coulomb_tile, diagonal):
@@ -31,7 +42,7 @@
     col_width = orbitals.shape[1]
     orbital_width = col_width * band_count
     piece_rows = blk // devices
-    all_points = lax.all_gather(orbitals, "grp", axis=0, tiled=True)
+    all_points = turned_line(orbitals, "grp", 0)
     block_count = all_points.shape[0] // (devices * piece_rows)
     blocks = (
         all_points.reshape(devices, block_count, piece_rows, col_width)

time: 1250 us -> 1180 us (0.944)
  waiting for transfers between devices: 532 us -> 439 us
  local copies, waits for them, and re-layouts: 196 us -> 213 us
    all_gather x1 -> x0, waiting for transfers between devices: 168 us -> none  [body(): all_points = lax.all_gather(orbitals, 'grp', axis=0, tiled=True)]
    ppermute x0 -> x3, waiting for transfers between devices: none -> 75.5 us  [turned_line(): terms = [lax.ppermute(terms[0], axis, right), *terms]]
  transfers between devices with their start and end apart: 3 -> 5, of which waited for: 3 -> 5; matrix products, arithmetic and copies ran while one was open for 0% -> 1% of each run, Pallas kernels for 0% -> 0%
where the time goes in v1:
time: 1180 us; the launch traced here: 1170 us
  waiting for transfers between devices  439 us (37%)
  matrix products  233 us (20%)
  local copies, waits for them, and re-layouts  213 us (18%)
  blocking collectives  211 us (18%)
  loops' own time  29 us (2%)
  other arithmetic  25.3 us (2%)
  between operations  13.8 us (1%)
    all_to_all x1, blocking collectives, body(): lax.all_to_all(outbound, 'band', split_axis=0, concat_axis=0, tiled=True)  211 us
    all_to_all x1, waiting for transfers between devices, body(): lax.all_to_all(outgoing, 'band', split_axis=0, concat_axis=0, tiled=True)  206 us
    reduce_scatter x1, waiting for transfers between devices, body(): mine = lax.psum_scatter(summed, 'grp', scatter_dimension=1, tiled=True)  158 us
    dot_general x3, matrix products, slot_work(): jnp.dot(kernel.T, first_block, precision=lax.Precision.HIGHEST, preferred...  98.7 us
    ppermute x3, waiting for transfers between devices, turned_line(): terms = [lax.ppermute(terms[0], axis, right), *terms]  75.5 us
    dot_general x3, matrix products, slot_work(): jnp.dot(first_block, second_block.T, precision=lax.Precision.HIGHEST, pre...  68 us
    squeeze x6, local copies, waits for them, and re-layouts, body(): results = lax.map(per_slot, (fetched, coulomb, diagonal))  53.1 us
    dot_general x3, matrix products, slot_work(): jnp.dot(kernel, second_block, precision=lax.Precision.HIGHEST, preferred_...  51.1 us
  transfers between devices with their start and end apart: 5, of which 5 were waited for; matrix products, arithmetic and copies ran while one was open for 1% of the time, Pallas kernels for 0%

profile of v1, /device:TPU:0, one launch (start us, length us, event | category | flops | bytes accessed | tf_op | source)
XLA Modules:
  0.0 1173.2 jit_solution(761536043164368507)
XLA Ops:
  9.6 28.2 %collective-permute-done = f32[4608,64]{0,1:T(8,128)S(1)} collective-permute-done((f32[4608,64]{0,1:T(8,128)}, f32[4608,64]{0,1:T(8,128)S(1)}, u32[]{:S(2)}, u32[]{:S(2)}) %collective-permute-start) | collective-permute-done | bytes 1179680 | tf_op jit(solution)/shard_map/ppermute | solution.py:12
  37.8 29.1 %collective-permute-done.1 = f32[4608,64]{0,1:T(8,128)} collective-permute-done((f32[4608,64]{0,1:T(8,128)S(1)}, f32[4608,64]{0,1:T(8,128)}, u32[]{:S(2)}, u32[]{:S(2)}) %collective-permute-start.1) | collective-permute-done | bytes 1179680 | tf_op jit(solution)/shard_map/ppermute | solution.py:12
  76.9 18.3 %collective-permute-done.2 = f32[4608,64]{0,1:T(8,128)} collective-permute-done((f32[4608,64]{0,1:T(8,128)}, f32[4608,64]{0,1:T(8,128)}, u32[]{:S(2)}, u32[]{:S(2)}) %collective-permute-start.2) | collective-permute-done | bytes 1179680 | tf_op jit(solution)/shard_map/ppermute | solution.py:12
  107.1 12.0 %copy.54 = f32[12,32,48,64]{2,1,3,0:T(8,128)} copy(f32[12,32,48,64]{3,2,0,1:T(8,128)} %bitcast.86) | data formatting | bytes 9437184 | tf_op jit(solution)/shard_map/transpose | solution.py:49
  119.1 13.1 %reshape.38 = f32[12,1536,64]{1,2,0:T(8,128)} reshape(f32[12,32,48,64]{2,1,3,0:T(8,128)} %copy.54) | data formatting | bytes 9437184 | tf_op jit(solution)/shard_map/reshape | solution.py:50
  132.2 12.6 %gather_fusion = f32[48,1536,64]{1,2,0:T(8,128)} fusion(f32[12,1536,64]{1,2,0:T(8,128)} %reshape.38, s32[1024]{0:T(1024)S(1)} %pad_clamp_fusion), kind=kCustom, calls=%fused_computation | custom fusion | bytes 37748928 | tf_op jit(solution)/shard_map/jit(_take)/gather | solution.py:57
  144.9 13.2 %select_multiply_fusion = f32[8,6,1536,64]{2,3,1,0:T(8,128)} fusion(f32[8,6,1536,64]{2,3,1,0:T(8,128)} %bitcast.84, f32[8,6]{1,0:T(8,128)S(1)} %copy.56, pred[8,6]{1,0:T(8,128)(4,1)S(1)} %copy.45), kind=kLoop, calls=%fused_computation.18 | loop fusion | flops 9437184 | bytes 37748976 | tf_op jit(solution)/shard_map/mul | solution.py:57
  164.7 205.9 %all-to-all-done = f32[8,6,1536,64]{2,3,1,0:T(8,128)} async-done(((f32[8,6,1536,64]{2,3,1,0:T(8,128)}), f32[8,6,1536,64]{2,3,1,0:T(8,128)}, u32[]{:S(2)}, u32[]{:S(2)}) %all-to-all-start) | async-done | bytes 18874400 | tf_op jit(solution)/shard_map/all_to_all | solution.py:58
  370.5 12.6 %copy.57 = f32[6,1536,8,64]{1,3,2,0:T(8,128)} copy(f32[6,1536,8,64]{1,3,0,2:T(8,128)} %bitcast.12) | data formatting | bytes 37748736 | tf_op jit(solution)/shard_map/transpose | solution.py:59
  383.1 359.8 %while.10 = (s32[]{:T(128)}, f32[3,2,1536,512]{2,3,1,0:T(8,128)}, f32[3,2,1536,512]{2,3,1,0:T(8,128)}, pred[3]{0:T(512)(128)(4,1)S(1)}, f32[3,1536,1536]{2,1,0:T...) while((s32[]{:T(128)}, f32[3,2,1536,512]{2,3,1,0:T(8,128)}, ...), condition=%wide.region_1.2_spmd, body=%wide.region_0.1_spmd.sunk | while | flops 43498340352 | bytes 179310272 | solution.py:69
  421.8 22.7 %convolution_multiply_fusion.3 = f32[1536,1536]{1,0:T(8,128)S(1)} fusion(f32[1536,1536]{0,1:T(8,128)} %copy.80, pred[]{:T(512)} %bitcast.83, f32[3,2,1536,512]{2,3,1,0:T(8,128)} %get-tuple-element.113, s32[]{:T(128)} %get-tuple-element.101, s32[]{:T(128)S(6)} %add.54, f32[3,1536,1536]{2,1,0:T(8,128)} %get-tuple-element.115), kind=kOutput, calls=%fused_computation.1.clone.1 | convolution fusion | flops 14504951808 | bytes 34605060 | tf_op jit(solution)/shard_map/while/body/eval_jaxpr/dot_general | solution.py:19
  448.0 17.0 %convolution_bitcast_fusion.2 = f32[1,1536,512]{2,1,0:T(8,128)S(1)} fusion(f32[1536,1536]{1,0:T(8,128)S(1)} %convolution_multiply_fusion.3, f32[3,2,1536,512]{2,3,1,0:T(8,128)} %get-tuple-element.113, s32[]{:T(128)} %get-tuple-element.101, s32[]{:T(128)S(6)} %add.54), kind=kOutput, calls=%fused_computation.9.clone.1 | convolution fusion | flops 14495514624 | bytes 15729156 | tf_op jit(solution)/shard_map/while/body/eval_jaxpr/dot_general | solution.py:27
  465.6 32.9 %fusion.22 = f32[1,1536,512]{2,1,0:T(8,128)S(1)} fusion(f32[1536,1536]{1,0:T(8,128)} %copy-done, f32[3,2,1536,512]{2,3,1,0:T(8,128)} %get-tuple-element.113, s32[]{:T(128)} %get-tuple-element.101, f32[]{:T(128)S(6)} %select_n.60), kind=kOutput, calls=%fused_computation.8.clone.1 | convolution fusion | flops 14496301056 | bytes 15729156 | tf_op jit(solution)/shard_map/while/body/eval_jaxpr/dot_general | solution.py:30
  532.5 22.7 %convolution_multiply_fusion.3 = f32[1536,1536]{1,0:T(8,128)S(1)} fusion(f32[1536,1536]{0,1:T(8,128)} %copy.80, pred[]{:T(512)} %bitcast.83, f32[3,2,1536,512]{2,3,1,0:T(8,128)} %get-tuple-element.113, s32[]{:T(128)} %get-tuple-element.101, s32[]{:T(128)S(6)} %add.54, f32[3,1536,1536]{2,1,0:T(8,128)} %get-tuple-element.115), kind=kOutput, calls=%fused_computation.1.clone.1 | convolution fusion | flops 14504951808 | bytes 34605060 | tf_op jit(solution)/shard_map/while/body/eval_jaxpr/dot_general | solution.py:19
  558.8 17.0 %convolution_bitcast_fusion.2 = f32[1,1536,512]{2,1,0:T(8,128)S(1)} fusion(f32[1536,1536]{1,0:T(8,128)S(1)} %convolution_multiply_fusion.3, f32[3,2,1536,512]{2,3,1,0:T(8,128)} %get-tuple-element.113, s32[]{:T(128)} %get-tuple-element.101, s32[]{:T(128)S(6)} %add.54), kind=kOutput, calls=%fused_computation.9.clone.1 | convolution fusion | flops 14495514624 | bytes 15729156 | tf_op jit(solution)/shard_map/while/body/eval_jaxpr/dot_general | solution.py:27
  576.4 32.9 %fusion.22 = f32[1,1536,512]{2,1,0:T(8,128)S(1)} fusion(f32[1536,1536]{1,0:T(8,128)} %copy-done, f32[3,2,1536,512]{2,3,1,0:T(8,128)} %get-tuple-element.113, s32[]{:T(128)} %get-tuple-element.101, f32[]{:T(128)S(6)} %select_n.60), kind=kOutput, calls=%fused_computation.8.clone.1 | convolution fusion | flops 14496301056 | bytes 15729156 | tf_op jit(solution)/shard_map/while/body/eval_jaxpr/dot_general | solution.py:30
  643.4 22.7 %convolution_multiply_fusion.3 = f32[1536,1536]{1,0:T(8,128)S(1)} fusion(f32[1536,1536]{0,1:T(8,128)} %copy.80, pred[]{:T(512)} %bitcast.83, f32[3,2,1536,512]{2,3,1,0:T(8,128)} %get-tuple-element.113, s32[]{:T(128)} %get-tuple-element.101, s32[]{:T(128)S(6)} %add.54, f32[3,1536,1536]{2,1,0:T(8,128)} %get-tuple-element.115), kind=kOutput, calls=%fused_computation.1.clone.1 | convolution fusion | flops 14504951808 | bytes 34605060 | tf_op jit(solution)/shard_map/while/body/eval_jaxpr/dot_general | solution.py:19
  669.7 17.0 %convolution_bitcast_fusion.2 = f32[1,1536,512]{2,1,0:T(8,128)S(1)} fusion(f32[1536,1536]{1,0:T(8,128)S(1)} %convolution_multiply_fusion.3, f32[3,2,1536,512]{2,3,1,0:T(8,128)} %get-tuple-element.113, s32[]{:T(128)} %get-tuple-element.101, s32[]{:T(128)S(6)} %add.54), kind=kOutput, calls=%fused_computation.9.clone.1 | convolution fusion | flops 14495514624 | bytes 15729156 | tf_op jit(solution)/shard_map/while/body/eval_jaxpr/dot_general | solution.py:27
  687.2 32.9 %fusion.22 = f32[1,1536,512]{2,1,0:T(8,128)S(1)} fusion(f32[1536,1536]{1,0:T(8,128)} %copy-done, f32[3,2,1536,512]{2,3,1,0:T(8,128)} %get-tuple-element.113, s32[]{:T(128)} %get-tuple-element.101, f32[]{:T(128)S(6)} %select_n.60), kind=kOutput, calls=%fused_computation.8.clone.1 | convolution fusion | flops 14496301056 | bytes 15729156 | tf_op jit(solution)/shard_map/while/body/eval_jaxpr/dot_general | solution.py:30
  742.9 12.6 %copy.60 = f32[8,6,1536,64]{2,3,1,0:T(8,128)} copy(f32[8,6,1536,64]{2,3,0,1:T(8,128)} %bitcast.87) | data formatting | bytes 37748736 | tf_op jit(solution)/shard_map/transpose | solution.py:70
  755.5 210.7 %all_to_all.10 = f32[8,6,1536,64]{2,3,1,0:T(8,128)S(1)} all-to-all(f32[8,6,1536,64]{2,3,1,0:T(8,128)} %copy.60), channel_id=1, replica_groups=mesh['grp'=4,'band'=8] {'band'}, dimensions={0} | all-to-all | bytes 37748736 | tf_op jit(solution)/shard_map/all_to_all | solution.py:71
  966.3 15.2 %fusion.8 = f32[12,1536,64]{1,0,2:T(8,128)} fusion(f32[8,6,1536,64]{2,3,1,0:T(8,128)S(1)} %all_to_all.10, s32[8,6]{0,1:T(8,128)S(1)} %copy-done.5), kind=kOutput, calls=%fused_computation.19 | convolution fusion | flops 679477824 | bytes 23593152 | tf_op jit(solution)/shard_map/srk,srpc->kpc/dot_general | solution.py:75
  992.5 12.2 %copy.63 = f32[12,4,8,48,64]{4,3,2,0,1:T(8,128)} copy(f32[12,4,8,48,64]{3,2,1,0,4:T(8,128)} %reshape.57) | data formatting | bytes 9437184 | tf_op jit(solution)/shard_map/reshape | solution.py:76
  1004.8 157.8 %reduce-scatter.2.cloned.1.call-done = f32[12,1,8,48,64]{4,3,2,0,1:T(8,128)} async-done(((f32[12,4,8,48,64]{4,3,2,0,1:T(8,128)}), f32[12,1,8,48,64]{4,3,2,0,1:T(8,128)}) %reduce-scatter.2.cloned.1.call-update) | async-done | bytes 1179664 | tf_op jit(solution)/shard_map/reduce_scatter | solution.py:77
  (70 shorter events, 159.1 us)
Async XLA Ops:
  6.5 31.2 %collective-permute-start = (f32[4608,64]{0,1:T(8,128)}, f32[4608,64]{0,1:T(8,128)S(1)}, u32[]{:S(2)}, u32[]{:S(2)}) collective-permute-start(f32[4608,64]{0,1:T(8,128)} %param.5), channel_id=1, source_target_pairs={{0,8},{8,16},{16,24},{24,0},{1,9},{9,17},{17,25},{25,1},{2,10},{10... | collective-permute-start | bytes 3538952 | tf_op jit(solution)/shard_map/ppermute | solution.py:12
  37.8 29.1 %collective-permute-start.1 = (f32[4608,64]{0,1:T(8,128)S(1)}, f32[4608,64]{0,1:T(8,128)}, u32[]{:S(2)}, u32[]{:S(2)}) collective-permute-start(f32[4608,64]{0,1:T(8,128)S(1)} %collective-permute-done), channel_id=1, source_target_pairs={{0,8},{8,16},{16,24},{24,0},{1,9},{9,17},{17,25},{25,1},{2,10},{10... | collective-permute-start | bytes 3538952 | tf_op jit(solution)/shard_map/ppermute | solution.py:12
  66.8 28.3 %collective-permute-start.2 = (f32[4608,64]{0,1:T(8,128)}, f32[4608,64]{0,1:T(8,128)}, u32[]{:S(2)}, u32[]{:S(2)}) collective-permute-start(f32[4608,64]{0,1:T(8,128)} %collective-permute-done.1), channel_id=1, source_target_pairs={{0,8},{8,16},{16,24},{24,0},{1,9},{9,17},{17,25},{25,1},{2,10},{10... | collective-permute-start | bytes 3538952 | tf_op jit(solution)/shard_map/ppermute | solution.py:12
  70.0 32.0 %copy-start.4 = (s32[8,6]{0,1:T(8,128)}, s32[8,6]{0,1:T(8,128)S(1)}, u32[]{:S(2)}) copy-start(s32[8,6]{0,1:T(8,128)S(1)} %get-tuple-element.59) | copy-start | bytes 580
  98.0 4.0 copy-start.1
  98.0 4.3 copy-start.3
  100.0 2.8 copy-start.2
  158.1 6.1 copy-start.6
  158.1 212.4 %all-to-all-start = ((f32[8,6,1536,64]{2,3,1,0:T(8,128)}), f32[8,6,1536,64]{2,3,1,0:T(8,128)}, u32[]{:S(2)}, u32[]{:S(2)}) async-start(f32[8,6,1536,64]{2,3,1,0:T(8,128)} %select_multiply_fusion), calls=%async_computation | async-start | bytes 37748736 | tf_op jit(solution)/shard_map/all_to_all | solution.py:58
  164.1 998.4 %reduce-scatter.2.cloned.1.call-start = ((), (), s32[]{:S(2)}) async-start(), calls=%async_computation.3 | async-start | bytes 11796480 | tf_op jit(solution)/shard_map/reduce_scatter | solution.py:77
  444.4 3.6 copy-start
  555.2 3.6 copy-start
  666.1 3.6 copy-start
  755.5 210.7 %copy-start.5 = (s32[8,6]{0,1:T(8,128)S(1)}, s32[8,6]{0,1:T(8,128)}, u32[]{:S(2)}) copy-start(s32[8,6]{0,1:T(8,128)} %copy-done.4) | copy-start | bytes 580
Sparse Core Ops, SparseCore 0:
  1004.9 157.6 reduce-scatter.1
